TPU v7x, 512 devices: a whole 4x8x8 slice. The times are simulated.
512 devices in a mesh: grp: 16 (over z, core), shard: 32 (over x, y).
Axes of the slice: x: 4, y: 8, z: 8, core: 2. Of those that a mesh axis runs over, the one named last changes fastest.
Arguments:
- src_rows: bfloat16 [128, 128, 5376], P('grp', 'shard'), may hold values from -6 to 6
- src_act: bfloat16 [128, 128], P('grp', 'shard'), may hold values from 0.29882812 to 3
- encoder: bfloat16 [16, 32, 3, 5376, 128], P('grp', 'shard'), may hold values from -0.078125 to 0.078125
- dest_list: int32 [16, 6], replicated, may hold values from -1 to 127, as said below
- pair_list: int32 [16, 32, 18, 2], P('grp', 'shard'), may hold values from 0 to 5, as said below
- pair_count: int32 [16, 32], P('grp', 'shard'), may hold values from 1 to 18, as said below
Outputs:
- edges: bfloat16 [16, 32, 18, 128, 128], P('grp', 'shard')
Inputs may be any that keep to these rules, and one draw needn't show every extreme that they name: `dest_list`: row g holds between 3 and 6 source blocks followed by -1; the blocks of one row come from distinct source groups (block // 8); some row is full. `pair_list`: entries are (slot, encoder block) with slot < 6 and block < 3; the first pair_count entries of a device are distinct pairs whose slot holds a block of its group. `pair_count`: at most 3 times the number of blocks of the device's group; some device has 18.
All inputs are finite; a program needn't handle non-finite values.
Results may differ from a plain program's by a relative error of at most 0.001.
Values may be sent and summed in bfloat16 or wider, within the bound.
No kernel may reach another device: no remote copies, remote signals or barrier semaphores. Data moves between devices by JAX's collectives and lax.ppermute only.
A program may use at most 64 MiB of HBM per device.

v0:
```python
import jax
import jax.numpy as jnp
from jax import lax
from jax.sharding import PartitionSpec as P


def local(src_rows, src_act, encoder, dest_list, pair_list, pair_count):
    my_group = lax.axis_index("grp")
    my_list = lax.dynamic_index_in_dim(dest_list, my_group, 0, keepdims=False)
    is_valid = my_list >= 0
    picked = jnp.maximum(my_list, 0)
    all_rows, all_scale = (
        lax.all_gather(src_rows, "grp", axis=0, tiled=True),
        lax.all_gather(src_act, "grp", axis=0, tiled=True),
    )
    slot_rows = jnp.take(all_rows, picked, axis=0)
    slot_scale = jnp.take(all_scale, picked, axis=0)
    slot_rows = jnp.where(is_valid[:, None, None], slot_rows, jnp.zeros((), slot_rows.dtype))
    slot_scale = jnp.where(is_valid[:, None], slot_scale, jnp.zeros((), slot_scale.dtype))
    full_rows, full_scale = (
        lax.all_gather(slot_rows, "shard", axis=1, tiled=True),
        lax.all_gather(slot_scale, "shard", axis=1, tiled=True),
    )
    weights = encoder[0, 0]
    dev_pairs = pair_list[0, 0]
    slot_ids = dev_pairs[:, 0]
    block_ids = dev_pairs[:, 1]
    amount = pair_count[0, 0]
    slots_total = full_rows.shape[0]
    tile_rows = full_rows.shape[1]
    width = full_rows.shape[2]
    enc_count = weights.shape[0]
    tile_cols = weights.shape[2]
    pair_total = dev_pairs.shape[0]
    stacked = full_rows.reshape(slots_total * tile_rows, width)
    products = jnp.einsum("rd,edc->rec", stacked, weights, preferred_element_type=jnp.float32)
    products = products.reshape(slots_total, tile_rows, enc_count, tile_cols)
    chosen = products[slot_ids, :, block_ids, :]
    scales = jnp.take(full_scale, slot_ids, axis=0).astype(jnp.float32)
    is_live = jnp.arange(pair_total) < amount
    result = jnp.where(
        is_live[:, None, None], scales[:, :, None] * chosen, jnp.zeros((), jnp.float32)
    ).astype(jnp.bfloat16)
    return result[None, None]


def solution(mesh):
    return jax.shard_map(
        local,
        mesh=mesh,
        in_specs=(
            P("grp", "shard", None),
            P("grp", "shard"),
            P("grp", "shard", None, None, None),
            P(),
            P("grp", "shard", None, None),
            P("grp", "shard"),
        ),
        out_specs=P("grp", "shard", None, None, None),
        check_vma=False,
    )
```

profile of v0, /device:TPU:1, one launch (start us, length us, event | category | flops | bytes accessed | tf_op | source)
XLA Modules:
  0.0 197.3 jit_solution(8817233090064426488)
XLA Ops:
  6.5 0.0 copy-start
  6.5 0.0 all-gather.5.cloned.1.call-start
  6.5 0.7 all-gather.5.cloned.1.call-update
  7.3 0.0 copy-start.1
  7.3 0.0 all-gather.7.cloned.1.call-start
  7.3 0.9 maximum_reduce_fusion
  8.2 0.9 compare_reduce_fusion.1
  9.1 53.5 %all-gather.5.cloned.1.call-done = bf16[128,4,5376]{2,1,0:T(4,128)(2,1)} async-done(((bf16[8,4,5376]{2,1,0:T(4,128)(2,1)}), bf16[128,4,5376]{2,1,0:T(4,128)(2,1)}) %all-gather.5.cloned.1.call-update) | async-done | bytes 5505040 | tf_op jit(solution)/shard_map/all_gather | solution.py:13
  62.6 3.3 %gather_fusion.2 = bf16[6,4,5376]{2,1,0:T(4,128)(2,1)S(1)} fusion(bf16[128,4,5376]{2,1,0:T(4,128)(2,1)} %all-gather.5.cloned.1.call-done, s32[1024]{0:T(1024)S(1)} %pad_clamp_fusion.1), kind=kCustom, calls=%fused_computation.2 | custom fusion | bytes 516120 | tf_op jit(solution)/shard_map/jit(_take)/gather | solution.py:16
  65.9 0.2 select_select_fusion
  66.2 0.8 copy.16
  66.9 0.0 all-gather.7.cloned.1.call-update
  67.0 0.0 copy-done
  67.0 16.3 %all-gather = bf16[16,8,4]{1,2,0:T(4,128)(2,1)S(1)} all-gather(bf16[1,8,4]{1,2,0:T(4,128)(2,1)S(1)} %bitcast.32), channel_id=1, replica_groups=mesh['grp'=16,'shard'=32] {'grp'}, dimensions={0}, use_global_device_ids=true | all-gather | bytes 1088 | tf_op jit(solution)/shard_map/all_gather | solution.py:14
  83.3 0.2 copy.13
  83.5 0.6 gather_fusion
  84.0 0.1 select_bitcast_fusion
  84.1 0.1 copy.14
  84.2 33.3 %all-gather.1 = bf16[32,4,6]{2,1,0:T(4,128)(2,1)S(1)} all-gather(bf16[1,4,6]{2,1,0:T(4,128)(2,1)S(1)} %bitcast.31), channel_id=1, replica_groups=mesh['grp'=16,'shard'=32] {'shard'}, dimensions={0}, use_global_device_ids=true | all-gather | bytes 1584 | tf_op jit(solution)/shard_map/all_gather | solution.py:22
  117.5 0.1 copy.19
  118.2 0.0 copy-done.1
  118.3 0.6 gather_fusion.1
  118.9 0.1 select_convert_fusion
  118.9 61.3 %all-gather.7.cloned.1.call-done = bf16[6,128,5376]{2,0,1:T(8,128)(2,1)} async-done(((bf16[6,4,5376]{2,0,1:T(8,128)(2,1)}), bf16[6,128,5376]{2,0,1:T(8,128)(2,1)}) %all-gather.7.cloned.1.call-update) | async-done | bytes 8257552 | tf_op jit(solution)/shard_map/all_gather | solution.py:21
  180.2 8.4 %fusion = f32[6,128,3,128]{3,1,2,0:T(8,128)S(1)} fusion(bf16[6,128,5376,1]{2,0,1,3:T(8,128)(2,1)} %bitcast.35, bf16[1,1,3,5376,128]{4,3,2,1,0:T(8,128)(2,1)} %param.8), kind=kOutput, calls=%fused_computation.4 | convolution fusion | flops 3170893824 | bytes 13565952 | tf_op jit(solution)/shard_map/rd,edc->rec/dot_general | solution.py:36
  188.6 0.7 gather_fusion.3
  189.3 1.2 fusion.4
  (5 shorter events, 0.0 us)
Async XLA Ops:
  6.5 60.4 %copy-start = (bf16[8,4]{0,1:T(4,128)(2,1)S(1)}, bf16[8,4]{0,1:T(4,128)(2,1)}, u32[]{:S(2)}) copy-start(bf16[8,4]{0,1:T(4,128)(2,1)} %param.7) | copy-start | bytes 196
  6.5 56.1 %all-gather.5.cloned.1.call-start = ((), (), s32[]{:S(2)}) async-start(), calls=%async_computation | async-start | bytes 5849088 | tf_op jit(solution)/shard_map/all_gather | solution.py:13
  7.3 111.0 %copy-start.1 = (s32[1,1,18,2]{2,3,1,0:T(2,128)S(1)}, s32[1,1,18,2]{2,3,1,0:T(2,128)}, u32[]{:S(2)}) copy-start(s32[1,1,18,2]{2,3,1,0:T(2,128)} %param.10) | copy-start | bytes 436
  7.3 172.9 %all-gather.7.cloned.1.call-start = ((), (), s32[]{:S(2)}) async-start(), calls=%async_computation.1 | async-start | bytes 11354112 | tf_op jit(solution)/shard_map/all_gather | solution.py:21
Sparse Core Ops, SparseCore 0:
  9.5 53.1 all-gather.4
  67.1 113.0 all-gather.6
where the time goes:
time: 198 us; the launch traced here: 197 us
  waiting for transfers between devices  115 us (58%)
  blocking collectives  49.6 us (25%)
  between operations  14.2 us (7%)
  matrix products  8.42 us (4%)
  local copies, waits for them, and re-layouts  6.26 us (3%)
  other arithmetic  3.4 us (2%)
    all_gather x1, waiting for transfers between devices, local(): lax.all_gather(slot_rows, 'shard', axis=1, tiled=True)  61.3 us
    all_gather x1, waiting for transfers between devices, local(): lax.all_gather(src_rows, 'grp', axis=0, tiled=True)  53.5 us
    all_gather x1, blocking collectives, local(): lax.all_gather(slot_scale, 'shard', axis=1, tiled=True)  33.3 us
    all_gather x1, blocking collectives, local(): lax.all_gather(src_act, 'grp', axis=0, tiled=True)  16.3 us
    dot_general x1, matrix products, local(): jnp.einsum('rd,edc->rec', stacked, weights, preferred_element_type=jnp.fl...  8.42 us
  transfers between devices with their start and end apart: 2, of which 2 were waited for; matrix products, arithmetic and copies ran while one was open for 2% of the time, Pallas kernels for 0%

commit v1 on v0

--- a/solution.py
+++ b/solution.py
@@ -18,7 +18,9 @@
     slot_rows = jnp.where(is_valid[:, None, None], slot_rows, jnp.zeros((), slot_rows.dtype))
     slot_scale = jnp.where(is_valid[:, None], slot_scale, jnp.zeros((), slot_scale.dtype))
     full_rows, full_scale = (
-        lax.all_gather(slot_rows, "shard", axis=1, tiled=True),
+        jnp.concatenate(
+            lax.all_to_all(jnp.stack([slot_rows] * lax.axis_size("shard")), "shard", 0, 0), axis=1
+        ),
         lax.all_gather(slot_scale, "shard", axis=1, tiled=True),
     )
     weights = encoder[0, 0]

time: 198 us -> 347 us (1.75); the launches traced: 197 us -> 342 us
  blocking collectives: 49.6 us -> 220 us
  waiting for transfers between devices: 115 us -> 54.3 us
  local copies, waits for them, and re-layouts: 6.26 us -> 31.7 us
  starting transfers between devices: 0.04 us -> 9.5 us
    all_gather x1, blocking collectives: 33.3 us -> 204 us  [local(): lax.all_gather(slot_scale, 'shard', axis=1, tiled=True)]
    all_gather x1 -> x0, waiting for transfers between devices: 61.3 us -> none  [local(): lax.all_gather(slot_rows, 'shard', axis=1, tiled=True)]
    dot_general x0 -> x1, local copies, waits for them, and re-layouts: none -> 12.9 us  [local(): jnp.einsum('rd,edc->rec', stacked, weights, preferred_element_type=jnp.fl...]
    all_to_all x0 -> x1, starting transfers between devices: none -> 9.5 us  [local(): lax.all_to_all(jnp.stack([slot_rows] * lax.axis_size('shard')), 'shard',...]
    reshape x0 -> x1, local copies, waits for them, and re-layouts: none -> 8.05 us  [local(): jnp.concatenate(lax.all_to_all(jnp.stack([slot_rows] * lax.axis_size('sha...]
    another operation x0 -> x1, local copies, waits for them, and re-layouts: none -> 5.31 us  [local(): jnp.stack([slot_rows] * lax.axis_size('shard'))]
  transfers between devices with their start and end apart: 2 -> 2, of which waited for: 2 -> 1; matrix products, arithmetic and copies ran while one was open for 2% -> 1% of each run, Pallas kernels for 0% -> 0%
where the time goes in v1:
time: 347 us; the launch traced here: 342 us
  blocking collectives  220 us (63%)
  waiting for transfers between devices  54.3 us (16%)
  local copies, waits for them, and re-layouts  31.7 us (9%)
  between operations  14.2 us (4%)
  starting transfers between devices  9.5 us (3%)
  matrix products  8.04 us (2%)
    all_gather x1, blocking collectives, local(): lax.all_gather(slot_scale, 'shard', axis=1, tiled=True)  204 us
    all_gather x1, waiting for transfers between devices, local(): lax.all_gather(src_rows, 'grp', axis=0, tiled=True)  53.6 us
    all_gather x1, blocking collectives, local(): lax.all_gather(src_act, 'grp', axis=0, tiled=True)  16.6 us
    dot_general x1, local copies, waits for them, and re-layouts, local(): jnp.einsum('rd,edc->rec', stacked, weights, preferred_element_type=jnp.fl...  12.9 us
    all_to_all x1, starting transfers between devices, local(): lax.all_to_all(jnp.stack([slot_rows] * lax.axis_size('shard')), 'shard',...  9.5 us
    reshape x1, local copies, waits for them, and re-layouts, local(): jnp.concatenate(lax.all_to_all(jnp.stack([slot_rows] * lax.axis_size('sha...  8.05 us
    dot_general x1, matrix products, local(): jnp.einsum('rd,edc->rec', stacked, weights, preferred_element_type=jnp.fl...  8.04 us
  transfers between devices with their start and end apart: 2, of which 1 were waited for; matrix products, arithmetic and copies ran while one was open for 1% of the time, Pallas kernels for 0%

profile of v1, /device:TPU:1, one launch (start us, length us, event | category | flops | bytes accessed | tf_op | source)
XLA Modules:
  0.0 341.6 jit_solution(13191892886071272160)
XLA Ops:
  6.5 0.0 all-gather.4.cloned.1.call-start
  6.5 0.7 all-gather.4.cloned.1.call-update
  7.3 0.9 maximum_reduce_fusion
  8.1 0.9 compare_reduce_fusion.1
  9.1 53.6 %all-gather.4.cloned.1.call-done = bf16[128,4,5376]{2,1,0:T(4,128)(2,1)} async-done(((bf16[8,4,5376]{2,1,0:T(4,128)(2,1)}), bf16[128,4,5376]{2,1,0:T(4,128)(2,1)}) %all-gather.4.cloned.1.call-update) | async-done | bytes 5505040 | tf_op jit(solution)/shard_map/all_gather | solution.py:13
  62.6 3.3 gather_fusion.2
  65.9 0.2 select_select_fusion
  66.2 5.3 %stack.2 = bf16[32,6,4,5376]{3,2,1,0:T(4,128)(2,1)} broadcast(bf16[6,4,5376]{2,1,0:T(4,128)(2,1)S(1)} %select_select_fusion), dimensions={1,2,3} | broadcast | bytes 8515584 | tf_op jit(solution)/shard_map/stack | solution.py:22
  71.5 0.0 copy-start
  71.5 0.0 copy-start.1
  71.5 9.5 %all-to-all-start = ((bf16[32,6,4,5376]{3,2,1,0:T(4,128)(2,1)}), bf16[32,6,4,5376]{3,2,1,0:T(4,128)(2,1)}, u32[]{:S(2)}, u32[]{:S(2)}) async-start(bf16[32,6,4,5376]{3,2,1,0:T(4,128)(2,1)} %stack.2), calls=%async_computation | async-start | bytes 16515072 | tf_op jit(solution)/shard_map/all_to_all | solution.py:22
  81.0 0.0 copy-done
  81.0 16.6 %all-gather = bf16[16,8,4]{1,2,0:T(4,128)(2,1)S(1)} all-gather(bf16[1,8,4]{1,2,0:T(4,128)(2,1)S(1)} %bitcast.35), channel_id=1, replica_groups=mesh['grp'=16,'shard'=32] {'grp'}, dimensions={0}, use_global_device_ids=true | all-gather | bytes 1088 | tf_op jit(solution)/shard_map/all_gather | solution.py:14
  97.6 0.2 copy.13
  97.8 0.6 gather_fusion
  98.3 0.1 select_bitcast_fusion
  98.4 0.1 copy.14
  98.5 203.9 %all-gather.1 = bf16[32,4,6]{2,1,0:T(4,128)(2,1)S(1)} all-gather(bf16[1,4,6]{2,1,0:T(4,128)(2,1)S(1)} %bitcast.34), channel_id=1, replica_groups=mesh['grp'=16,'shard'=32] {'shard'}, dimensions={0}, use_global_device_ids=true | all-gather | bytes 1584 | tf_op jit(solution)/shard_map/all_gather | solution.py:24
  302.4 0.1 copy.18
  303.2 0.0 copy-done.1
  303.2 0.6 gather_fusion.1
  303.8 0.1 select_convert_fusion
  303.9 0.0 all-to-all-done
  303.9 8.1 %copy.16 = bf16[6,32,4,5376]{3,2,1,0:T(4,128)(2,1)} copy(bf16[6,32,4,5376]{3,2,0,1:T(4,128)(2,1)} %bitcast.10) | data formatting | bytes 16515072 | tf_op jit(solution)/shard_map/reshape | solution.py:21
  311.9 12.9 %reshape.120 = bf16[6,128,5376,1]{2,1,0,3:T(8,128)(2,1)} reshape(bf16[6,32,4,5376]{3,2,1,0:T(4,128)(2,1)} %copy.16) | data formatting | bytes 16515072 | tf_op jit(solution)/shard_map/rd,edc->rec/dot_general | solution.py:38
  324.8 8.0 %fusion = f32[6,128,3,128]{3,1,2,0:T(8,128)S(1)} fusion(bf16[6,128,5376,1]{2,1,0,3:T(8,128)(2,1)} %reshape.120, bf16[1,1,3,5376,128]{4,3,2,1,0:T(8,128)(2,1)} %param.8), kind=kOutput, calls=%fused_computation.4 | convolution fusion | flops 3170893824 | bytes 13565952 | tf_op jit(solution)/shard_map/rd,edc->rec/dot_general | solution.py:38
  332.9 0.7 gather_fusion.3
  333.5 1.2 fusion.4
  (5 shorter events, 0.0 us)
Async XLA Ops:
  6.5 56.1 %all-gather.4.cloned.1.call-start = ((), (), s32[]{:S(2)}) async-start(), calls=%async_computation.1 | async-start | bytes 5849088 | tf_op jit(solution)/shard_map/all_gather | solution.py:13
  71.5 9.5 %copy-start = (bf16[8,4]{0,1:T(4,128)(2,1)S(1)}, bf16[8,4]{0,1:T(4,128)(2,1)}, u32[]{:S(2)}) copy-start(bf16[8,4]{0,1:T(4,128)(2,1)} %param.7) | copy-start | bytes 196
  71.5 231.7 %copy-start.1 = (s32[1,1,18,2]{2,3,1,0:T(2,128)S(1)}, s32[1,1,18,2]{2,3,1,0:T(2,128)}, u32[]{:S(2)}) copy-start(s32[1,1,18,2]{2,3,1,0:T(2,128)} %param.10) | copy-start | bytes 436
  71.5 232.4 %all-to-all-start = ((bf16[32,6,4,5376]{3,2,1,0:T(4,128)(2,1)}), bf16[32,6,4,5376]{3,2,1,0:T(4,128)(2,1)}, u32[]{:S(2)}, u32[]{:S(2)}) async-start(bf16[32,6,4,5376]{3,2,1,0:T(4,128)(2,1)} %stack.2), calls=%async_computation | async-start | bytes 16515072 | tf_op jit(solution)/shard_map/all_to_all | solution.py:22
Sparse Core Ops, SparseCore 0:
  9.5 53.1 all-gather.3
